TPU v7x, 256 devices: a whole 4x4x8 slice. The times are simulated.
256 devices in a mesh: lat: 8 (over y, z_lo), lon: 8 (over x, core), dp: 4 (over z_hi).
Axes of the slice: x: 4, y: 4, z: 8 (z_hi: 4, z_lo: 2; z = z_hi * 2 + z_lo), core: 2. Of those that a mesh axis runs over, the one named last changes fastest.
Arguments:
- state_grid: bfloat16 [4, 384, 768, 128], P('dp', ('lat', 'lon')), may hold values from -6 to 6
- cotangent: bfloat16 [4, 384, 768, 128], P('dp', ('lat', 'lon')), may hold values from -6 to 6
- legendre: bfloat16 [384, 384, 384], P(('lat', 'lon')), may hold values from -0.3125 to 0.3125
- wave_ids: int32 [384], replicated, may hold values from 0 to 383, each once
- weights: bfloat16 [384, 2, 4, 1024], P('lat'), may hold values from -0.75 to 0.75
Outputs:
- input_grad: bfloat16 [4, 384, 768, 128], P('dp', ('lat', 'lon'))
- weight_grad: float32 [384, 2, 4, 1024], P('lat')
Inputs may be any that keep to these rules, and one draw needn't show every extreme that they name: wave_ids[j] is the wavenumber of slot j; each of 0 to 383 stands in exactly one slot.
All inputs are finite; a program needn't handle non-finite values.
Results may differ from a plain program's by a relative error of at most 0.034.
Values may be sent and summed in bfloat16 or wider, within the bound.
No kernel may reach another device: no remote copies, remote signals or barrier semaphores. Data moves between devices by JAX's collectives and lax.ppermute only.
A program may use at most 128 MiB of HBM per device.

v0:
```python
import math
import jax
import jax.numpy as jnp
from jax import lax
from jax.sharding import PartitionSpec as P

NLON = 768
GROUPS = 4
GROUP_WIDTH = 32


def build_tables(wave_ids):
    columns = jnp.arange(NLON, dtype=jnp.int32)
    phase_int = wave_ids[:, None] * columns[None, :] % NLON
    angles = phase_int.astype(jnp.float32) * jnp.float32(2.0 * math.pi / NLON)
    factor = jnp.float32(1.0 / math.sqrt(NLON))
    paired = jnp.stack([jnp.cos(angles) * factor, -jnp.sin(angles) * factor], axis=1)
    forward_table = paired.reshape(2 * wave_ids.shape[0], NLON)
    doubling = jnp.where(wave_ids == 0, 1.0, 2.0).astype(jnp.float32)
    inverse_table = forward_table * jnp.repeat(doubling, 2)[:, None]
    return (forward_table.astype(jnp.bfloat16), inverse_table.astype(jnp.bfloat16))


def build_kernel(weights):
    degree_count = weights.shape[0]
    real_part = weights[:, 0].reshape(degree_count, GROUPS, GROUP_WIDTH, GROUP_WIDTH)
    imag_part = weights[:, 1].reshape(degree_count, GROUPS, GROUP_WIDTH, GROUP_WIDTH)
    upper_rows = jnp.stack([real_part, imag_part], axis=3)
    lower_rows = jnp.stack([-imag_part, real_part], axis=3)
    return jnp.stack([upper_rows, lower_rows], axis=2)


def gelu_slope(branch):
    normal_cdf = 0.5 * (1.0 + lax.erf(branch * (1.0 / math.sqrt(2.0))))
    density = jnp.exp(-0.5 * branch * branch) * (1.0 / math.sqrt(2.0 * math.pi))
    return normal_cdf + branch * density


def shards(state_grid, cotangent, legendre, wave_ids, weights):
    lat_count = lax.axis_size("lat")
    lon_count = lax.axis_size("lon")
    samples, rows_dev, lon_cells, channels = state_grid.shape
    slot_count, lat_cells, degree_count = legendre.shape
    slot_reals = 2 * slot_count
    first_slot = (lax.axis_index("lat") * lon_count + lax.axis_index("lon")) * slot_count
    held_waves = lax.dynamic_slice_in_dim(wave_ids, first_slot, slot_count)
    degree_ids = jnp.arange(degree_count, dtype=jnp.int32)
    masked = jnp.where(
        degree_ids[None, None, :] >= held_waves[:, None, None],
        legendre,
        jnp.zeros((), legendre.dtype),
    )
    slot_order = wave_ids.reshape(lat_count, lon_count, slot_count).transpose(1, 0, 2).reshape(-1)
    forward_table, inverse_table = build_tables(slot_order)
    kernel = build_kernel(weights)

    def analyze(source, twiddle):
        spectra = jnp.einsum(
            "srnc,kn->srkc", source, twiddle, preferred_element_type=jnp.float32
        ).astype(jnp.bfloat16)
        gathered = lax.all_to_all(
            lax.all_to_all(spectra, "lon", split_axis=2, concat_axis=1, tiled=True),
            "lat",
            split_axis=2,
            concat_axis=1,
            tiled=True,
        )
        blocks = gathered.reshape(samples, lat_cells, slot_count, 2 * channels)
        spectral = jnp.einsum("samc,mal->slmc", blocks, masked, preferred_element_type=jnp.float32)
        spectral = spectral.astype(jnp.bfloat16).reshape(
            samples, degree_count, slot_reals, channels
        )
        return lax.all_to_all(spectral, "lat", split_axis=1, concat_axis=2, tiled=True)

    def synthesize(spectral, twiddle):
        joined = lax.all_to_all(spectral, "lat", split_axis=2, concat_axis=1, tiled=True)
        blocks = joined.reshape(samples, degree_count, slot_count, 2 * channels)
        spectra = jnp.einsum(
            "slmc,mal->samc", blocks, masked, preferred_element_type=jnp.float32
        ).astype(jnp.bfloat16)
        spectra = spectra.reshape(samples, lat_cells, slot_reals, channels)
        pencil = lax.all_to_all(
            lax.all_to_all(spectra, "lat", split_axis=1, concat_axis=2, tiled=True),
            "lon",
            split_axis=1,
            concat_axis=2,
            tiled=True,
        )
        return jnp.einsum("srkc,kn->srnc", pencil, twiddle, preferred_element_type=jnp.float32)

    def split_groups(spectral):
        return spectral.reshape(samples, spectral.shape[1], -1, 2, GROUPS, GROUP_WIDTH)

    coef_fwd = analyze(state_grid, forward_table)
    coef_six = split_groups(coef_fwd)
    mixed_coef = jnp.einsum(
        "slmpgi,lgpiqo->slmqgo", coef_six, kernel, preferred_element_type=jnp.float32
    ).astype(jnp.bfloat16)
    branch = synthesize(mixed_coef.reshape(coef_fwd.shape), inverse_table)
    pulled = (cotangent.astype(jnp.float32) * gelu_slope(branch)).astype(jnp.bfloat16)
    back_coef = analyze(pulled, inverse_table)
    back_six = split_groups(back_coef)
    outer_sums = jnp.einsum(
        "slmpgi,slmqgo->lgpiqo", coef_six, back_six, preferred_element_type=jnp.float32
    )
    real_grad = outer_sums[:, :, 0, :, 0, :] + outer_sums[:, :, 1, :, 1, :]
    imag_grad = outer_sums[:, :, 0, :, 1, :] - outer_sums[:, :, 1, :, 0, :]
    local_grad = jnp.stack([real_grad, imag_grad], axis=1).reshape(weights.shape)
    weight_grad = lax.psum(local_grad.astype(jnp.bfloat16), ("lon", "dp")).astype(jnp.float32)
    demixed = jnp.einsum(
        "slmqgo,lgpiqo->slmpgi", back_six, kernel, preferred_element_type=jnp.float32
    ).astype(jnp.bfloat16)
    returned = synthesize(demixed.reshape(back_coef.shape), forward_table)
    input_grad = (cotangent.astype(jnp.float32) + returned).astype(jnp.bfloat16)
    return (input_grad, weight_grad)


def solution(mesh):
    return jax.shard_map(
        shards,
        mesh=mesh,
        in_specs=(
            P("dp", ("lat", "lon"), None, None),
            P("dp", ("lat", "lon"), None, None),
            P(("lat", "lon"), None, None),
            P(),
            P("lat", None, None, None),
        ),
        out_specs=(P("dp", ("lat", "lon"), None, None), P("lat", None, None, None)),
        check_vma=False,
    )
```

profile of v0, /device:TPU:8, one launch (start us, length us, event | category | flops | bytes accessed | tf_op | source)
XLA Modules:
  0.0 725.3 jit_solution(13457028617643623277)
XLA Ops:
  8.2 4.9 cosine_multiply_fusion
  22.5 25.9 %all_to_all.192 = bf16[1,6,768,128]{3,1,0,2:T(8,128)(2,1)S(1)} all-to-all(bf16[1,6,768,128]{3,1,0,2:T(8,128)(2,1)S(1)} %copy.223), channel_id=1, replica_groups=mesh['lat'=8,'lon'=8,'dp'=4] {'lon'}, dimensions={2} | all-to-all | bytes 2359296 | tf_op jit(solution)/shard_map/all_to_all | solution.py:62
  50.1 6.5 all-to-all-start.1
  57.4 13.8 %all-to-all-done.1 = bf16[1,48,96,128]{3,1,0,2:T(8,128)(2,1)S(1)} async-done(((bf16[1,48,96,128]{3,1,0,2:T(8,128)(2,1)}), bf16[1,48,96,128]{3,1,0,2:T(8,128)(2,1)S(1)}, u32[]{:S(2)}, u32[]{:S(2)}) %all-to-all-start.1) | async-done | bytes 1179680 | tf_op jit(solution)/shard_map/all_to_all | solution.py:61
  74.2 4.4 reshape.378
  85.0 6.4 all-to-all-start.2
  103.2 12.7 %copy.232 = bf16[48,4,2,32,2,32]{3,5,2,4,1,0:T(8,128)(2,1)} copy(bf16[48,4,2,32,2,32]{0,5,4,3,1,2:T(8,128)(2,1)} %pad_maximum_fusion) | data formatting | bytes 3145728 | tf_op jit(solution)/shard_map/stack | solution.py:30
  120.3 8.3 %copy.270 = bf16[48,48,2,4,32,1]{1,4,2,5,3,0:T(8,128)(2,1)} copy(bf16[48,48,2,4,32,1]{0,4,3,2,1,5:T(8,128)(2,1)} %bitcast.179) | data formatting | bytes 2359296 | tf_op jit(solution)/shard_map/reshape.8
  128.5 6.7 fusion
  135.3 8.3 %copy.234 = bf16[1,48,48,2,4,32]{1,5,4,3,2,0:T(8,128)(2,1)} copy(bf16[1,48,48,2,4,32]{2,5,3,4,1,0:T(8,128)(2,1)} %fusion) | data formatting | bytes 2359296 | tf_op jit(solution)/shard_map/convert_element_type | solution.py:98
  146.7 19.4 %all_to_all.193 = bf16[1,48,96,128]{3,1,0,2:T(8,128)(2,1)} all-to-all(bf16[1,48,96,128]{3,1,0,2:T(8,128)(2,1)S(1)} %copy.235), channel_id=1, replica_groups=mesh['lat'=8,'lon'=8,'dp'=4] {'lat'}, dimensions={2} | all-to-all | bytes 2359296 | tf_op jit(solution)/shard_map/all_to_all | solution.py:76
  170.4 4.4 reshape.379
  181.2 21.5 %all_to_all.194 = bf16[1,384,12,128]{3,2,0,1:T(8,128)(2,1)S(1)} all-to-all(bf16[1,384,12,128]{3,2,0,1:T(8,128)(2,1)} %copy.238), channel_id=1, replica_groups=mesh['lat'=8,'lon'=8,'dp'=4] {'lat'}, dimensions={1} | all-to-all | bytes 2359296 | tf_op jit(solution)/shard_map/all_to_all | solution.py:83
  204.4 4.3 all-to-all-start.5
  211.1 14.9 %all-to-all-done.5 = bf16[1,48,96,128]{3,2,0,1:T(8,128)(2,1)} async-done(((bf16[1,48,96,128]{3,2,0,1:T(8,128)(2,1)}), bf16[1,48,96,128]{3,2,0,1:T(8,128)(2,1)}, u32[]{:S(2)}, u32[]{:S(2)}) %all-to-all-start.5) | async-done | bytes 1179680 | tf_op jit(solution)/shard_map/all_to_all | solution.py:82
  227.4 4.8 fusion.15
  234.4 24.2 %all_to_all.195 = bf16[1,6,768,128]{3,1,0,2:T(8,128)(2,1)S(1)} all-to-all(bf16[1,6,768,128]{3,1,0,2:T(8,128)(2,1)S(1)} %copy.244), channel_id=1, replica_groups=mesh['lat'=8,'lon'=8,'dp'=4] {'lon'}, dimensions={2} | all-to-all | bytes 2359296 | tf_op jit(solution)/shard_map/all_to_all | solution.py:62
  259.3 20.1 %all_to_all.196 = bf16[1,48,96,128]{3,1,0,2:T(8,128)(2,1)S(1)} all-to-all(bf16[1,48,96,128]{3,1,0,2:T(8,128)(2,1)S(1)} %copy.247), channel_id=1, replica_groups=mesh['lat'=8,'lon'=8,'dp'=4] {'lat'}, dimensions={2} | all-to-all | bytes 2359296 | tf_op jit(solution)/shard_map/all_to_all | solution.py:61
  282.4 4.4 reshape.380
  291.1 5.1 all-to-all-start.8
  296.3 11.6 %copy.253 = bf16[48,4,2,32,2,32]{5,3,4,2,1,0:T(8,128)(2,1)} copy(bf16[48,4,2,32,2,32]{0,5,4,3,1,2:T(8,128)(2,1)} %pad_maximum_fusion) | data formatting | bytes 3145728 | tf_op jit(solution)/shard_map/stack | solution.py:30
  307.8 6.3 all-to-all-done.8
  317.2 8.3 %copy.273 = bf16[48,48,2,4,32,1]{1,4,2,5,3,0:T(8,128)(2,1)} copy(bf16[48,48,2,4,32,1]{0,4,3,2,1,5:T(8,128)(2,1)} %bitcast.182) | data formatting | bytes 2359296 | tf_op jit(solution)/shard_map/reshape.39
  325.5 6.8 fusion.1
  332.3 8.3 %copy.255 = bf16[1,48,48,2,4,32]{1,5,4,3,2,0:T(8,128)(2,1)} copy(bf16[1,48,48,2,4,32]{2,5,3,4,1,0:T(8,128)(2,1)} %fusion.1) | data formatting | bytes 2359296 | tf_op jit(solution)/shard_map/convert_element_type | solution.py:112
  343.8 19.7 %all_to_all.197 = bf16[1,48,96,128]{3,1,0,2:T(8,128)(2,1)S(1)} all-to-all(bf16[1,48,96,128]{3,1,0,2:T(8,128)(2,1)S(1)} %copy.256), channel_id=1, replica_groups=mesh['lat'=8,'lon'=8,'dp'=4] {'lat'}, dimensions={2} | all-to-all | bytes 2359296 | tf_op jit(solution)/shard_map/all_to_all | solution.py:76
  366.4 4.4 reshape.381
  375.3 5.3 all-to-all-start.10
  380.6 8.3 %copy.276 = bf16[48,48,2,4,32,1]{1,4,5,2,3,0:T(8,128)(2,1)} copy(bf16[48,48,2,4,32,1]{0,4,3,2,1,5:T(8,128)(2,1)} %bitcast.180) | data formatting | bytes 2359296 | tf_op jit(solution)/shard_map/reshape.8
  388.9 12.5 %fusion.41 = f32[48,4,2,32,2,32]{5,3,4,2,1,0:T(8,128)} fusion(bf16[48,48,2,4,32,1]{1,4,5,2,3,0:T(8,128)(2,1)} %copy.276, bf16[48,48,2,4,32,1]{1,4,2,5,3,0:T(8,128)(2,1)} %copy.273), kind=kOutput, calls=%fused_computation.66 | convolution fusion | flops 75497472 | bytes 5505024 | tf_op jit(solution)/shard_map/slmpgi,slmqgo->lgpiqo/dot_general | solution.py:103
  407.4 7.5 %fusion.3 = (bf16[48,4,1,32,1,32]{5,3,4,2,1,0:T(8,128)(2,1)}, bf16[48,4,1,32,1,32]{5,3,4,2,1,0:T(8,128)(2,1)S(1)}) fusion(f32[48,4,2,32,2,32]{5,3,4,2,1,0:T(8,128)} %fusion.41), kind=kLoop, calls=%fused_computation.9 | loop fusion | flops 786432 | bytes 3932160 | tf_op jit(solution)/shard_map/convert.3
  421.6 290.0 %all-reduce.2.cloned.1.call-done = bf16[48,2,4,1024]{3,0,2,1:T(8,128)(2,1)} async-done(((bf16[48,2,4,1024]{3,0,2,1:T(8,128)(2,1)}), bf16[48,2,4,1024]{3,0,2,1:T(8,128)(2,1)}) %all-reduce.2.cloned.1.call-update) | async-done | bytes 786448 | tf_op jit(solution)/shard_map/psum | solution.py:109
  (78 shorter events, 100.5 us)
Async XLA Ops:
  7.2 12.2 %copy-start = (bf16[1,6,768,128]{3,2,1,0:T(8,128)(2,1)S(1)}, bf16[1,6,768,128]{3,2,1,0:T(8,128)(2,1)}, u32[]{:S(2)}) copy-start(bf16[1,6,768,128]{3,2,1,0:T(8,128)(2,1)} %param.5) | copy-start | bytes 3538948
  50.1 21.1 %all-to-all-start.1 = ((bf16[1,48,96,128]{3,1,0,2:T(8,128)(2,1)}), bf16[1,48,96,128]{3,1,0,2:T(8,128)(2,1)S(1)}, u32[]{:S(2)}, u32[]{:S(2)}) async-start(bf16[1,48,96,128]{3,1,0,2:T(8,128)(2,1)} %copy.226), calls=%async_computation.1 | async-start | bytes 2359296 | tf_op jit(solution)/shard_map/all_to_all | solution.py:61
  85.0 6.4 copy-start.3
  85.0 30.9 %all-to-all-start.2 = ((bf16[1,384,12,128]{3,2,0,1:T(8,128)(2,1)}), bf16[1,384,12,128]{3,2,0,1:T(8,128)(2,1)}, u32[]{:S(2)}, u32[]{:S(2)}) async-start(bf16[1,384,12,128]{3,2,0,1:T(8,128)(2,1)} %copy.229), calls=%async_computation.2 | async-start | bytes 3145728 | tf_op jit(solution)/shard_map/all_to_all | solution.py:73
  204.4 21.6 %all-to-all-start.5 = ((bf16[1,48,96,128]{3,2,0,1:T(8,128)(2,1)}), bf16[1,48,96,128]{3,2,0,1:T(8,128)(2,1)}, u32[]{:S(2)}, u32[]{:S(2)}) async-start(bf16[1,48,96,128]{3,2,0,1:T(8,128)(2,1)} %copy.241), calls=%async_computation.5 | async-start | bytes 2359296 | tf_op jit(solution)/shard_map/all_to_all | solution.py:82
  291.1 23.0 %all-to-all-start.8 = ((bf16[1,384,12,128]{3,2,0,1:T(8,128)(2,1)}), bf16[1,384,12,128]{3,2,0,1:T(8,128)(2,1)S(1)}, u32[]{:S(2)}, u32[]{:S(2)}) async-start(bf16[1,384,12,128]{3,2,0,1:T(8,128)(2,1)} %copy.250), calls=%async_computation.8 | async-start | bytes 3145728 | tf_op jit(solution)/shard_map/all_to_all | solution.py:73
  375.3 26.1 %all-to-all-start.10 = ((bf16[1,384,12,128]{3,2,0,1:T(8,128)(2,1)}), bf16[1,384,12,128]{3,2,0,1:T(8,128)(2,1)S(1)}, u32[]{:S(2)}, u32[]{:S(2)}) async-start(bf16[1,384,12,128]{3,2,0,1:T(8,128)(2,1)} %copy.259), calls=%async_computation.10 | async-start | bytes 3145728 | tf_op jit(solution)/shard_map/all_to_all | solution.py:83
  403.1 311.3 %all-to-all-start.11 = ((bf16[1,48,96,128]{3,2,0,1:T(8,128)(2,1)}), bf16[1,48,96,128]{3,2,0,1:T(8,128)(2,1)}, u32[]{:S(2)}, u32[]{:S(2)}) async-start(bf16[1,48,96,128]{3,2,0,1:T(8,128)(2,1)} %copy.262), calls=%async_computation.11 | async-start | bytes 2359296 | tf_op jit(solution)/shard_map/all_to_all | solution.py:82
  407.4 304.2 %all-reduce.2.cloned.1.call-start = ((), (), s32[]{:S(2)}) async-start(), calls=%async_computation.12 | async-start | bytes 1572864 | tf_op jit(solution)/shard_map/psum | solution.py:109
  419.5 1.6 copy-start.2
  714.5 1.6 copy-start.4
  716.1 2.1 copy-start.1
Sparse Core Ops, SparseCore 0:
  420.8 290.7 all-reduce.1
where the time goes:
time: 735 us; the launch traced here: 725 us
  waiting for transfers between devices  325 us (44%)
  local copies, waits for them, and re-layouts  155 us (21%)
  blocking collectives  131 us (18%)
  matrix products  47 us (6%)
  starting transfers between devices  31.8 us (4%)
  other arithmetic  20.7 us (3%)
  between operations  14.6 us (2%)
    psum x1, waiting for transfers between devices, shards(): lax.psum(local_grad.astype(jnp.bfloat16), ('lon', 'dp')).astype(jnp.float32)  290 us
    another operation x11, local copies, waits for them, and re-layouts  55.7 us
    all_to_all x2, blocking collectives, analyze(): lax.all_to_all(spectra, 'lon', split_axis=2, concat_axis=1, tiled=True)  50.1 us
    all_to_all x2, blocking collectives, synthesize(): lax.all_to_all(spectral, 'lat', split_axis=2, concat_axis=1, tiled=True)  39.1 us
    another operation x2, local copies, waits for them, and re-layouts, build_kernel(): return jnp.stack([upper_rows, lower_rows], axis=2)  24.2 us
    all_to_all x1, blocking collectives, synthesize(): lax.all_to_all(spectra, 'lat', split_axis=1, concat_axis=2, tiled=True)  21.5 us
    all_to_all x1, blocking collectives, analyze(): lax.all_to_all(lax.all_to_all(spectra, 'lon', split_axis=2, concat_axis=1...  20.1 us
    all_to_all x2, waiting for transfers between devices, synthesize(): lax.all_to_all(lax.all_to_all(spectra, 'lat', split_axis=1, concat_axis=2...  14.9 us
  transfers between devices with their start and end apart: 7, of which 4 were waited for; matrix products, arithmetic and copies ran while one was open for 11% of the time, Pallas kernels for 0%

commit v1 on v0

--- a/solution.py
+++ b/solution.py
@@ -106,7 +106,9 @@
     real_grad = outer_sums[:, :, 0, :, 0, :] + outer_sums[:, :, 1, :, 1, :]
     imag_grad = outer_sums[:, :, 0, :, 1, :] - outer_sums[:, :, 1, :, 0, :]
     local_grad = jnp.stack([real_grad, imag_grad], axis=1).reshape(weights.shape)
-    weight_grad = lax.psum(local_grad.astype(jnp.bfloat16), ("lon", "dp")).astype(jnp.float32)
+    weight_grad = jnp.sum(
+        lax.all_gather(local_grad.astype(jnp.bfloat16), ("lon", "dp")), axis=0
+    ).astype(jnp.float32)
     demixed = jnp.einsum(
         "slmqgo,lgpiqo->slmpgi", back_six, kernel, preferred_element_type=jnp.float32
     ).astype(jnp.bfloat16)

time: 735 us -> 561 us (0.76)
  waiting for transfers between devices: 325 us -> 62.1 us
  blocking collectives: 131 us -> 220 us
  other arithmetic: 20.7 us -> 29.3 us
    psum x1 -> x0, waiting for transfers between devices: 290 us -> none  [shards(): lax.psum(local_grad.astype(jnp.bfloat16), ('lon', 'dp')).astype(jnp.float32)]
    all_to_all x1 -> x2, blocking collectives: 21.5 us -> 105 us  [synthesize(): lax.all_to_all(spectra, 'lat', split_axis=1, concat_axis=2, tiled=True)]
    all_to_all x2, waiting for transfers between devices: 14.9 us -> 39.1 us  [synthesize(): lax.all_to_all(lax.all_to_all(spectra, 'lat', split_axis=1, concat_axis=2...]
    reduce_sum x0 -> x1, other arithmetic: none -> 13.5 us  [shards(): jnp.sum(lax.all_gather(local_grad.astype(jnp.bfloat16), ('lon', 'dp')), a...]
    another operation x11 -> x15, local copies, waits for them, and re-layouts: 55.7 us -> 60.6 us
  transfers between devices with their start and end apart: 7 -> 6, of which waited for: 4 -> 4; matrix products, arithmetic and copies ran while one was open for 11% -> 15% of each run, Pallas kernels for 0% -> 0%
where the time goes in v1:
time: 561 us; the launch traced here: 550 us
  blocking collectives  220 us (39%)
  local copies, waits for them, and re-layouts  154 us (27%)
  waiting for transfers between devices  62.1 us (11%)
  matrix products  42.5 us (8%)
  other arithmetic  29.3 us (5%)
  starting transfers between devices  27.1 us (5%)
  between operations  14.6 us (3%)
    all_to_all x2, blocking collectives, synthesize(): lax.all_to_all(spectra, 'lat', split_axis=1, concat_axis=2, tiled=True)  105 us
    another operation x11, local copies, waits for them, and re-layouts  55.9 us
    all_to_all x2, blocking collectives, analyze(): lax.all_to_all(spectra, 'lon', split_axis=2, concat_axis=1, tiled=True)  50.1 us
    all_to_all x2, blocking collectives, synthesize(): lax.all_to_all(spectral, 'lat', split_axis=2, concat_axis=1, tiled=True)  45 us
    all_to_all x2, waiting for transfers between devices, synthesize(): lax.all_to_all(lax.all_to_all(spectra, 'lat', split_axis=1, concat_axis=2...  39.1 us
    another operation x2, local copies, waits for them, and re-layouts, build_kernel(): return jnp.stack([upper_rows, lower_rows], axis=2)  24.4 us
    all_to_all x1, blocking collectives, analyze(): lax.all_to_all(lax.all_to_all(spectra, 'lon', split_axis=2, concat_axis=1...  19.7 us
    all_to_all x1, waiting for transfers between devices, analyze(): lax.all_to_all(lax.all_to_all(spectra, 'lon', split_axis=2, concat_axis=1...  13.8 us
  transfers between devices with their start and end apart: 6, of which 4 were waited for; matrix products, arithmetic and copies ran while one was open for 15% of the time, Pallas kernels for 0%

profile of v1, /device:TPU:8, one launch (start us, length us, event | category | flops | bytes accessed | tf_op | source)
XLA Modules:
  0.0 549.8 jit_solution(1014255720697731381)
XLA Ops:
  8.2 4.9 cosine_multiply_fusion
  22.5 25.9 %all_to_all.192 = bf16[1,6,768,128]{3,1,0,2:T(8,128)(2,1)S(1)} all-to-all(bf16[1,6,768,128]{3,1,0,2:T(8,128)(2,1)S(1)} %copy.220), channel_id=1, replica_groups=mesh['lat'=8,'lon'=8,'dp'=4] {'lon'}, dimensions={2} | all-to-all | bytes 2359296 | tf_op jit(solution)/shard_map/all_to_all | solution.py:62
  50.1 6.5 %all-to-all-start.1 = ((bf16[1,48,96,128]{3,1,0,2:T(8,128)(2,1)}), bf16[1,48,96,128]{3,1,0,2:T(8,128)(2,1)S(1)}, u32[]{:S(2)}, u32[]{:S(2)}) async-start(bf16[1,48,96,128]{3,1,0,2:T(8,128)(2,1)} %copy.223), calls=%async_computation.1 | async-start | bytes 2359296 | tf_op jit(solution)/shard_map/all_to_all | solution.py:61
  57.4 13.8 %all-to-all-done.1 = bf16[1,48,96,128]{3,1,0,2:T(8,128)(2,1)S(1)} async-done(((bf16[1,48,96,128]{3,1,0,2:T(8,128)(2,1)}), bf16[1,48,96,128]{3,1,0,2:T(8,128)(2,1)S(1)}, u32[]{:S(2)}, u32[]{:S(2)}) %all-to-all-start.1) | async-done | bytes 1179680 | tf_op jit(solution)/shard_map/all_to_all | solution.py:61
  74.2 4.4 reshape.421
  85.0 6.4 %all-to-all-start.2 = ((bf16[1,384,12,128]{3,2,0,1:T(8,128)(2,1)}), bf16[1,384,12,128]{3,2,0,1:T(8,128)(2,1)}, u32[]{:S(2)}, u32[]{:S(2)}) async-start(bf16[1,384,12,128]{3,2,0,1:T(8,128)(2,1)} %copy.226), calls=%async_computation.2 | async-start | bytes 3145728 | tf_op jit(solution)/shard_map/all_to_all | solution.py:73
  103.1 12.6 %copy.229 = bf16[48,4,2,32,2,32]{3,5,2,4,1,0:T(8,128)(2,1)} copy(bf16[48,4,2,32,2,32]{0,5,4,3,1,2:T(8,128)(2,1)} %pad_maximum_fusion) | data formatting | bytes 3145728 | tf_op jit(solution)/shard_map/stack | solution.py:30
  120.3 8.3 %copy.267 = bf16[48,48,2,4,32,1]{1,4,2,5,3,0:T(8,128)(2,1)} copy(bf16[48,48,2,4,32,1]{0,4,3,2,1,5:T(8,128)(2,1)} %bitcast.179) | data formatting | bytes 2359296 | tf_op jit(solution)/shard_map/reshape.8
  128.6 6.7 %fusion = bf16[1,48,48,2,4,32]{2,5,3,4,1,0:T(8,128)(2,1)} fusion(bf16[48,4,2,32,2,32]{3,5,2,4,1,0:T(8,128)(2,1)} %copy.229, bf16[48,48,2,4,32,1]{1,4,2,5,3,0:T(8,128)(2,1)} %copy.267), kind=kOutput, calls=%fused_computation.4 | convolution fusion | flops 76087296 | bytes 3932160 | tf_op jit(solution)/shard_map/slmpgi,lgpiqo->slmqgo/dot_general | solution.py:96
  135.3 8.3 %copy.231 = bf16[1,48,48,2,4,32]{1,5,4,3,2,0:T(8,128)(2,1)} copy(bf16[1,48,48,2,4,32]{2,5,3,4,1,0:T(8,128)(2,1)} %fusion) | data formatting | bytes 2359296 | tf_op jit(solution)/shard_map/convert_element_type | solution.py:98
  146.8 19.4 %all_to_all.193 = bf16[1,48,96,128]{3,1,0,2:T(8,128)(2,1)} all-to-all(bf16[1,48,96,128]{3,1,0,2:T(8,128)(2,1)S(1)} %copy.232), channel_id=1, replica_groups=mesh['lat'=8,'lon'=8,'dp'=4] {'lat'}, dimensions={2} | all-to-all | bytes 2359296 | tf_op jit(solution)/shard_map/all_to_all | solution.py:76
  170.4 4.4 reshape.422
  181.2 21.5 %all_to_all.194 = bf16[1,384,12,128]{3,2,0,1:T(8,128)(2,1)S(1)} all-to-all(bf16[1,384,12,128]{3,2,0,1:T(8,128)(2,1)} %copy.235), channel_id=1, replica_groups=mesh['lat'=8,'lon'=8,'dp'=4] {'lat'}, dimensions={1} | all-to-all | bytes 2359296 | tf_op jit(solution)/shard_map/all_to_all | solution.py:83
  211.2 14.9 %all-to-all-done.5 = bf16[1,48,96,128]{3,2,0,1:T(8,128)(2,1)} async-done(((bf16[1,48,96,128]{3,2,0,1:T(8,128)(2,1)}), bf16[1,48,96,128]{3,2,0,1:T(8,128)(2,1)}, u32[]{:S(2)}, u32[]{:S(2)}) %all-to-all-start.5) | async-done | bytes 1179680 | tf_op jit(solution)/shard_map/all_to_all | solution.py:82
  227.5 4.8 fusion.15
  234.4 24.2 %all_to_all.195 = bf16[1,6,768,128]{3,1,0,2:T(8,128)(2,1)S(1)} all-to-all(bf16[1,6,768,128]{3,1,0,2:T(8,128)(2,1)S(1)} %copy.241), channel_id=1, replica_groups=mesh['lat'=8,'lon'=8,'dp'=4] {'lon'}, dimensions={2} | all-to-all | bytes 2359296 | tf_op jit(solution)/shard_map/all_to_all | solution.py:62
  259.4 19.7 %all_to_all.196 = bf16[1,48,96,128]{3,1,0,2:T(8,128)(2,1)S(1)} all-to-all(bf16[1,48,96,128]{3,1,0,2:T(8,128)(2,1)S(1)} %copy.244), channel_id=1, replica_groups=mesh['lat'=8,'lon'=8,'dp'=4] {'lat'}, dimensions={2} | all-to-all | bytes 2359296 | tf_op jit(solution)/shard_map/all_to_all | solution.py:61
  282.0 4.4 reshape.423
  290.8 5.1 all-to-all-start.8
  296.3 8.3 %copy.273 = bf16[48,48,2,4,32,1]{1,4,5,2,3,0:T(8,128)(2,1)} copy(bf16[48,48,2,4,32,1]{0,4,3,2,1,5:T(8,128)(2,1)} %bitcast.180) | data formatting | bytes 2359296 | tf_op jit(solution)/shard_map/reshape.8
  304.6 9.2 %all-to-all-done.8 = bf16[1,384,12,128]{3,2,0,1:T(8,128)(2,1)S(1)} async-done(((bf16[1,384,12,128]{3,2,0,1:T(8,128)(2,1)}), bf16[1,384,12,128]{3,2,0,1:T(8,128)(2,1)S(1)}, u32[]{:S(2)}, u32[]{:S(2)}) %all-to-all-start.8) | async-done | bytes 1179680 | tf_op jit(solution)/shard_map/all_to_all | solution.py:73
  316.9 8.3 %copy.270 = bf16[48,48,2,4,32,1]{1,4,2,5,3,0:T(8,128)(2,1)} copy(bf16[48,48,2,4,32,1]{0,4,3,2,1,5:T(8,128)(2,1)} %bitcast.182) | data formatting | bytes 2359296 | tf_op jit(solution)/shard_map/reshape.39
  325.2 7.9 %fusion.41 = f32[48,4,2,32,2,32]{5,3,4,2,1,0:T(8,128)S(1)} fusion(bf16[48,48,2,4,32,1]{1,4,5,2,3,0:T(8,128)(2,1)} %copy.273, bf16[48,48,2,4,32,1]{1,4,2,5,3,0:T(8,128)(2,1)} %copy.270), kind=kOutput, calls=%fused_computation.66 | convolution fusion | flops 75497472 | bytes 5505024 | tf_op jit(solution)/shard_map/slmpgi,slmqgo->lgpiqo/dot_general | solution.py:103
  341.4 11.7 %copy.250 = bf16[48,4,2,32,2,32]{5,3,4,2,1,0:T(8,128)(2,1)} copy(bf16[48,4,2,32,2,32]{0,5,4,3,1,2:T(8,128)(2,1)} %pad_maximum_fusion) | data formatting | bytes 3145728 | tf_op jit(solution)/shard_map/stack | solution.py:30
  353.2 7.2 %fusion.1 = bf16[1,48,48,2,4,32]{2,5,3,4,1,0:T(8,128)(2,1)} fusion(bf16[48,4,2,32,2,32]{5,3,4,2,1,0:T(8,128)(2,1)} %copy.250, bf16[48,48,2,4,32,1]{1,4,2,5,3,0:T(8,128)(2,1)} %copy.270), kind=kOutput, calls=%fused_computation.5 | convolution fusion | flops 76087296 | bytes 3932160 | tf_op jit(solution)/shard_map/slmqgo,lgpiqo->slmpgi/dot_general | solution.py:112
  360.4 8.3 %copy.252 = bf16[1,48,48,2,4,32]{1,5,4,3,2,0:T(8,128)(2,1)} copy(bf16[1,48,48,2,4,32]{2,5,3,4,1,0:T(8,128)(2,1)} %fusion.1) | data formatting | bytes 2359296 | tf_op jit(solution)/shard_map/convert_element_type | solution.py:114
  371.9 25.5 %all_to_all.197 = bf16[1,48,96,128]{3,1,0,2:T(8,128)(2,1)S(1)} all-to-all(bf16[1,48,96,128]{3,1,0,2:T(8,128)(2,1)S(1)} %copy.253), channel_id=1, replica_groups=mesh['lat'=8,'lon'=8,'dp'=4] {'lat'}, dimensions={2} | all-to-all | bytes 2359296 | tf_op jit(solution)/shard_map/all_to_all | solution.py:76
  400.5 4.6 reshape.424
  409.4 83.8 %all_to_all.198 = bf16[1,384,12,128]{3,2,0,1:T(8,128)(2,1)S(1)} all-to-all(bf16[1,384,12,128]{3,2,0,1:T(8,128)(2,1)S(1)} %copy.256), channel_id=1, replica_groups=mesh['lat'=8,'lon'=8,'dp'=4] {'lat'}, dimensions={1} | all-to-all | bytes 2359296 | tf_op jit(solution)/shard_map/all_to_all | solution.py:83
  494.9 4.5 all-to-all-start.11
  499.9 24.2 %all-to-all-done.11 = bf16[1,48,96,128]{3,2,0,1:T(8,128)(2,1)S(1)} async-done(((bf16[1,48,96,128]{3,2,0,1:T(8,128)(2,1)}), bf16[1,48,96,128]{3,2,0,1:T(8,128)(2,1)S(1)}, u32[]{:S(2)}, u32[]{:S(2)}) %all-to-all-start.11) | async-done | bytes 1179680 | tf_op jit(solution)/shard_map/all_to_all | solution.py:82
  527.5 13.5 %reduce_sum.12 = bf16[48,2,4,1024]{3,0,2,1:T(8,128)(2,1)S(1)} reduce(bf16[32,48,2,4,1024]{4,1,3,2,0:T(8,128)(2,1)} %all-gather.2.cloned.1.call-done, bf16[]{:T(256)} %constant.15.clone.1), dimensions={0}, to_apply=%region_0.1 | reduce | flops 12189696 | bytes 25952258 | tf_op jit(solution)/shard_map/reduce_sum | solution.py:109
  (80 shorter events, 101.7 us)
Async XLA Ops:
  7.2 12.2 %copy-start = (bf16[1,6,768,128]{3,2,1,0:T(8,128)(2,1)S(1)}, bf16[1,6,768,128]{3,2,1,0:T(8,128)(2,1)}, u32[]{:S(2)}) copy-start(bf16[1,6,768,128]{3,2,1,0:T(8,128)(2,1)} %param.5) | copy-start | bytes 3538948
  50.1 21.1 %all-to-all-start.1 = ((bf16[1,48,96,128]{3,1,0,2:T(8,128)(2,1)}), bf16[1,48,96,128]{3,1,0,2:T(8,128)(2,1)S(1)}, u32[]{:S(2)}, u32[]{:S(2)}) async-start(bf16[1,48,96,128]{3,1,0,2:T(8,128)(2,1)} %copy.223), calls=%async_computation.1 | async-start | bytes 2359296 | tf_op jit(solution)/shard_map/all_to_all | solution.py:61
  85.0 6.4 %copy-start.3 = (bf16[48,2,4,1024]{3,2,1,0:T(4,128)(2,1)S(1)}, bf16[48,2,4,1024]{3,2,1,0:T(4,128)(2,1)}, u32[]{:S(2)}) copy-start(bf16[48,2,4,1024]{3,2,1,0:T(4,128)(2,1)} %param.9) | copy-start | bytes 2359300
  85.0 30.8 %all-to-all-start.2 = ((bf16[1,384,12,128]{3,2,0,1:T(8,128)(2,1)}), bf16[1,384,12,128]{3,2,0,1:T(8,128)(2,1)}, u32[]{:S(2)}, u32[]{:S(2)}) async-start(bf16[1,384,12,128]{3,2,0,1:T(8,128)(2,1)} %copy.226), calls=%async_computation.2 | async-start | bytes 3145728 | tf_op jit(solution)/shard_map/all_to_all | solution.py:73
  204.5 21.6 %all-to-all-start.5 = ((bf16[1,48,96,128]{3,2,0,1:T(8,128)(2,1)}), bf16[1,48,96,128]{3,2,0,1:T(8,128)(2,1)}, u32[]{:S(2)}, u32[]{:S(2)}) async-start(bf16[1,48,96,128]{3,2,0,1:T(8,128)(2,1)} %copy.238), calls=%async_computation.5 | async-start | bytes 2359296 | tf_op jit(solution)/shard_map/all_to_all | solution.py:82
  290.8 23.0 %all-to-all-start.8 = ((bf16[1,384,12,128]{3,2,0,1:T(8,128)(2,1)}), bf16[1,384,12,128]{3,2,0,1:T(8,128)(2,1)S(1)}, u32[]{:S(2)}, u32[]{:S(2)}) async-start(bf16[1,384,12,128]{3,2,0,1:T(8,128)(2,1)} %copy.247), calls=%async_computation.8 | async-start | bytes 3145728 | tf_op jit(solution)/shard_map/all_to_all | solution.py:73
  295.9 231.5 %all-gather.2.cloned.1.call-start = ((), (), s32[]{:S(2)}) async-start(), calls=%async_computation.12 | async-start | bytes 25952256 | tf_op jit(solution)/shard_map/all_gather | solution.py:110
  400.5 4.6 copy-start.4
  494.9 4.5 copy-start.2
  494.9 29.1 %all-to-all-start.11 = ((bf16[1,48,96,128]{3,2,0,1:T(8,128)(2,1)}), bf16[1,48,96,128]{3,2,0,1:T(8,128)(2,1)S(1)}, u32[]{:S(2)}, u32[]{:S(2)}) async-start(bf16[1,48,96,128]{3,2,0,1:T(8,128)(2,1)} %copy.259), calls=%async_computation.11 | async-start | bytes 2359296 | tf_op jit(solution)/shard_map/all_to_all | solution.py:82
  524.0 1.3 copy-start.5
  527.5 15.3 %copy-start.1 = (bf16[1,6,768,128]{3,2,1,0:T(8,128)(2,1)S(1)}, bf16[1,6,768,128]{3,2,1,0:T(8,128)(2,1)}, u32[]{:S(2)}) copy-start(bf16[1,6,768,128]{3,2,1,0:T(8,128)(2,1)} %param.5) | copy-start | bytes 3538948
Sparse Core Ops, SparseCore 0:
  341.6 180.9 all-gather.1
